TPU v7x, 32 devices: a whole 2x2x4 slice. The times are simulated.
32 devices in a mesh: segment: 2 (over core), expert: 16 (over z, y, x).
Axes of the slice: x: 2, y: 2, z: 4, core: 2. Of those that a mesh axis runs over, the one named last changes fastest.
Arguments:
- hidden_in: bfloat16 [2, 256, 7168], P('segment', 'expert'), may hold values from -6 to 6
- norm_gain: bfloat16 [2, 7168], P('segment'), may hold values from 0.25 to 1.75
- up_proj: bfloat16 [2, 8192, 7168], P('segment', 'expert'), may hold values from -0.0625 to 0.0625
- down_proj: bfloat16 [2, 8192, 7168], P('segment', 'expert'), may hold values from -0.1875 to 0.1875
- expert_ids: int32 [2, 256, 2], P('segment', 'expert'), may hold values from 0 to 7, all different within a row; in each aligned block of 16 rows (0 to 15, 16 to 31, ..., all dimensions but the last counted through in order) at most 7 rows name the same one
- gate_weights: float32 [2, 256, 2], P('segment', 'expert'), may hold values from 0.2 to 1
Outputs:
- handed_on: bfloat16 [2, 256, 7168], P('segment', 'expert')
Inputs may be any that keep to these rules, and one draw needn't show every extreme that they name: `expert_ids`: each row names 2 different experts. Among the rows of one device in one section no expert is named by more than 7 rows, and in some device an expert is named by exactly 7.
All inputs are finite; a program needn't handle non-finite values.
Results may differ from a plain program's by a relative error of at most 0.0075.
Values may be sent and summed in bfloat16 or wider, within the bound.
No kernel may reach another device: no remote copies, remote signals or barrier semaphores. Data moves between devices by JAX's collectives and lax.ppermute only.
A program may use at most 64 MiB of HBM per device.

v0:
```python
import jax
import jax.numpy as jnp
from jax import lax
from jax.sharding import PartitionSpec as P

EXPERTS = 8


def passed_along(shard, axis, by):
    count = lax.axis_size(axis)
    return lax.ppermute(shard, axis, [(i, (i + by) % count) for i in range(count)])


def shards(hidden_in, norm_gain, up_proj, down_proj, expert_ids, gate_weights):
    members = lax.axis_size("expert")
    me = lax.axis_index("expert")
    tokens = hidden_in[0]
    gain = norm_gain[0]
    up_block = up_proj[0]
    down_block = down_proj[0]
    local_units = up_block.shape[0]
    units_per_expert = local_units * members // EXPERTS
    my_expert = me * local_units // units_per_expert
    square = jnp.mean(tokens.astype(jnp.float32) ** 2, axis=-1, keepdims=True)
    normed = (
        tokens.astype(jnp.float32) * lax.rsqrt(square + 1e-06) * gain.astype(jnp.float32)
    ).astype(jnp.bfloat16)
    all_rows = lax.all_gather(normed, "expert", axis=0, tiled=True)
    all_ids = lax.all_gather(expert_ids[0], "expert", axis=0, tiled=True)
    all_gates = lax.all_gather(gate_weights[0], "expert", axis=0, tiled=True)
    scale = jnp.sum(jnp.where(all_ids == my_expert, all_gates, 0.0), axis=-1, keepdims=True)
    inner = jnp.einsum("rd,fd->rf", all_rows, up_block, preferred_element_type=jnp.float32)
    active = jax.nn.silu(inner).astype(jnp.bfloat16)
    partial = jnp.dot(active, down_block, preferred_element_type=jnp.float32).astype(jnp.bfloat16)
    contribution = partial.astype(jnp.float32) * scale
    mixture = lax.psum_scatter(contribution, "expert", scatter_dimension=0, tiled=True)
    section_out = (tokens.astype(jnp.float32) + mixture).astype(jnp.bfloat16)
    handed = passed_along(section_out, "segment", 1)
    return handed[None]


def solution(mesh):
    in_specs = (
        P("segment", "expert", None),
        P("segment", None),
        P("segment", "expert", None),
        P("segment", "expert", None),
        P("segment", "expert", None),
        P("segment", "expert", None),
    )
    out_specs = P("segment", "expert", None)
    return jax.shard_map(shards, mesh=mesh, in_specs=in_specs, out_specs=out_specs, check_vma=False)
```

profile of v0, /device:TPU:11, one launch (start us, length us, event | category | flops | bytes accessed | tf_op | source)
XLA Modules:
  0.0 272.6 jit_solution(9835408425453076009)
XLA Ops:
  6.5 0.0 all-gather.4.cloned.1.call-start
  6.5 1.1 fusion.9
  7.7 0.8 mul.46
  8.4 1.8 fusion.11
  10.2 0.0 all-gather.4.cloned.1.call-update
  10.2 0.0 reduce-scatter.2.cloned.1.call-start
  10.3 0.8 copy.7
  11.0 0.8 copy.8
  11.8 24.2 %all-gather.1 = f32[1,256,2]{2,0,1:T(1,128)S(1)} all-gather(f32[1,16,2]{2,0,1:T(1,128)S(1)} %copy.8), channel_id=3, replica_groups=mesh['segment'=2,'expert'=16] {'expert'}, dimensions={1}, use_global_device_ids=true | all-gather | bytes 2176 | tf_op jit(solution)/shard_map/all_gather | solution.py:30
  36.0 36.2 %all-gather = s32[1,256,2]{2,0,1:T(1,128)S(1)} all-gather(s32[1,16,2]{2,0,1:T(1,128)S(1)} %copy.7), channel_id=2, replica_groups=mesh['segment'=2,'expert'=16] {'expert'}, dimensions={1}, use_global_device_ids=true | all-gather | bytes 2176 | tf_op jit(solution)/shard_map/all_gather | solution.py:29
  72.1 1.0 fusion.14
  73.2 10.5 %all-gather.4.cloned.1.call-done = bf16[256,7168]{1,0:T(8,128)(2,1)} async-done(((bf16[16,7168]{1,0:T(8,128)(2,1)}), bf16[256,7168]{1,0:T(8,128)(2,1)}) %all-gather.4.cloned.1.call-update) | async-done | bytes 3670032 | tf_op jit(solution)/shard_map/all_gather | solution.py:28
  83.7 13.3 %fusion.1 = f32[256,7168]{1,0:T(8,128)} fusion(bf16[1,512,7168]{2,1,0:T(8,128)(2,1)} %param.9, f32[256]{0:T(256)S(1)} %fusion.14, bf16[256,7168]{1,0:T(8,128)(2,1)} %all-gather.4.cloned.1.call-done, bf16[1,512,7168]{2,1,0:T(8,128)(2,1)} %param.8), kind=kOutput, calls=%fused_computation.2 | convolution fusion | flops 3764256768 | bytes 25691136 | tf_op jit(solution)/shard_map/dot_general | solution.py:34
  97.0 0.0 copy-start
  97.0 0.0 reduce-scatter.2.cloned.1.call-update
  97.1 164.8 %reduce-scatter.2.cloned.1.call-done = f32[16,7168]{1,0:T(8,128)} async-done(((f32[256,7168]{1,0:T(8,128)}), f32[16,7168]{1,0:T(8,128)}) %reduce-scatter.2.cloned.1.call-update) | async-done | bytes 458768 | tf_op jit(solution)/shard_map/reduce_scatter | solution.py:36
  261.9 0.0 copy-done
  261.9 1.1 fusion.12
  263.0 1.0 collective-permute-start
  264.0 1.1 collective-permute-done
  265.1 0.7 copy.10
  (1 shorter events, 0.0 us)
Async XLA Ops:
  6.5 77.2 %all-gather.4.cloned.1.call-start = ((), (), s32[]{:S(2)}) async-start(), calls=%async_computation.1 | async-start | bytes 3899392 | tf_op jit(solution)/shard_map/all_gather | solution.py:28
  10.2 251.7 %reduce-scatter.2.cloned.1.call-start = ((), (), s32[]{:S(2)}) async-start(), calls=%async_computation.2 | async-start | bytes 7798784 | tf_op jit(solution)/shard_map/reduce_scatter | solution.py:36
  97.0 164.9 %copy-start = (bf16[1,16,7168]{2,1,0:T(8,128)(2,1)S(1)}, bf16[1,16,7168]{2,1,0:T(8,128)(2,1)}, u32[]{:S(2)}) copy-start(bf16[1,16,7168]{2,1,0:T(8,128)(2,1)} %param.6) | copy-start | bytes 688132
  263.0 2.2 collective-permute-start
Sparse Core Ops, SparseCore 0:
  10.3 73.3 all-gather.3
  97.2 164.6 reduce-scatter.1
where the time goes:
time: 273 us
  waiting for transfers between devices  176 us (64%)
  blocking collectives  60.4 us (22%)
  between operations  13.4 us (5%)
  matrix products  13.3 us (5%)
  other arithmetic  5.74 us (2%)
    reduce_scatter x1, waiting for transfers between devices, shards(): lax.psum_scatter(contribution, 'expert', scatter_dimension=0, tiled=True)  165 us
    all_gather x1, blocking collectives, shards(): all_ids = lax.all_gather(expert_ids[0], 'expert', axis=0, tiled=True)  36.2 us
    all_gather x1, blocking collectives, shards(): all_gates = lax.all_gather(gate_weights[0], 'expert', axis=0, tiled=True)  24.2 us
    dot_general x1, matrix products, shards(): jnp.dot(active, down_block, preferred_element_type=jnp.float32)  13.3 us
    all_gather x1, waiting for transfers between devices, shards(): all_rows = lax.all_gather(normed, 'expert', axis=0, tiled=True)  10.5 us
  transfers between devices with their start and end apart: 3, of which 3 were waited for; matrix products, arithmetic and copies ran while one was open for 1% of the time, Pallas kernels for 0%

commit v1 on v0

--- a/solution.py
+++ b/solution.py
@@ -26,7 +26,14 @@
         tokens.astype(jnp.float32) * lax.rsqrt(square + 1e-06) * gain.astype(jnp.float32)
     ).astype(jnp.bfloat16)
     all_rows = lax.all_gather(normed, "expert", axis=0, tiled=True)
-    all_ids = lax.all_gather(expert_ids[0], "expert", axis=0, tiled=True)
+    ring = [expert_ids[0]]
+    for hop in range(15):
+        ring.append(lax.ppermute(ring[-1], "expert", [(dev, (dev + 1) % 16) for dev in range(16)]))
+    all_ids = jnp.roll(
+        jnp.concatenate(ring[::-1], axis=0),
+        (lax.axis_index("expert") + 1) * ring[0].shape[0],
+        axis=0,
+    )
     all_gates = lax.all_gather(gate_weights[0], "expert", axis=0, tiled=True)
     scale = jnp.sum(jnp.where(all_ids == my_expert, all_gates, 0.0), axis=-1, keepdims=True)
     inner = jnp.einsum("rd,fd->rf", all_rows, up_block, preferred_element_type=jnp.float32)

time: 273 us -> 334 us (1.22)
  waiting for transfers between devices: 176 us -> 272 us
  blocking collectives: 60.4 us -> 24.2 us
    ppermute x0 -> x15, waiting for transfers between devices: none -> 71.3 us  [shards(): lax.ppermute(ring[-1], 'expert', [(dev, (dev + 1) % 16) for dev in range(...]
    all_gather x1 -> x0, blocking collectives: 36.2 us -> none  [shards(): all_ids = lax.all_gather(expert_ids[0], 'expert', axis=0, tiled=True)]
    reduce_scatter x1, waiting for transfers between devices: 165 us -> 199 us  [shards(): lax.psum_scatter(contribution, 'expert', scatter_dimension=0, tiled=True)]
    all_gather x1, waiting for transfers between devices: 10.5 us -> 0.02 us  [shards(): all_rows = lax.all_gather(normed, 'expert', axis=0, tiled=True)]
  transfers between devices with their start and end apart: 3 -> 18, of which waited for: 3 -> 16; matrix products, arithmetic and copies ran while one was open for 1% -> 1% of each run, Pallas kernels for 0% -> 0%
where the time goes in v1:
time: 334 us; the launch traced here: 333 us
  waiting for transfers between devices  272 us (81%)
  blocking collectives  24.2 us (7%)
  between operations  13.4 us (4%)
  matrix products  13.3 us (4%)
  other arithmetic  4.82 us (1%)
  starting transfers between devices  3.36 us (1%)
    reduce_scatter x1, waiting for transfers between devices, shards(): lax.psum_scatter(contribution, 'expert', scatter_dimension=0, tiled=True)  199 us
    ppermute x15, waiting for transfers between devices, shards(): lax.ppermute(ring[-1], 'expert', [(dev, (dev + 1) % 16) for dev in range(...  71.3 us
    all_gather x1, blocking collectives, shards(): all_gates = lax.all_gather(gate_weights[0], 'expert', axis=0, tiled=True)  24.2 us
    dot_general x1, matrix products, shards(): jnp.dot(active, down_block, preferred_element_type=jnp.float32)  13.3 us
  transfers between devices with their start and end apart: 18, of which 16 were waited for; matrix products, arithmetic and copies ran while one was open for 1% of the time, Pallas kernels for 0%

profile of v1, /device:TPU:11, one launch (start us, length us, event | category | flops | bytes accessed | tf_op | source)
XLA Modules:
  0.0 333.2 jit_solution(14297542240977863408)
XLA Ops:
  6.5 1.1 fusion.9
  8.4 1.8 fusion.11
  10.3 1.3 collective-permute-start
  12.3 24.2 %all-gather = f32[1,256,2]{2,0,1:T(1,128)S(1)} all-gather(f32[1,16,2]{2,0,1:T(1,128)S(1)} %copy.7), channel_id=2, replica_groups=mesh['segment'=2,'expert'=16] {'expert'}, dimensions={1}, use_global_device_ids=true | all-gather | bytes 2176 | tf_op jit(solution)/shard_map/all_gather | solution.py:37
  36.5 1.0 collective-permute-start.1
  37.5 4.1 %collective-permute-done.1 = s32[16,2]{0,1:T(2,128)S(1)} collective-permute-done((s32[16,2]{0,1:T(2,128)S(1)}, s32[16,2]{0,1:T(2,128)S(1)}, u32[]{:S(2)}, u32[]{:S(2)}) %collective-permute-start.1) | collective-permute-done | bytes 160 | tf_op jit(solution)/shard_map/ppermute | solution.py:31
  41.6 4.2 %collective-permute-done.2 = s32[16,2]{0,1:T(2,128)S(1)} collective-permute-done((s32[16,2]{0,1:T(2,128)S(1)}, s32[16,2]{0,1:T(2,128)S(1)}, u32[]{:S(2)}, u32[]{:S(2)}) %collective-permute-start.2) | collective-permute-done | bytes 160 | tf_op jit(solution)/shard_map/ppermute | solution.py:31
  45.8 4.0 %collective-permute-done.3 = s32[16,2]{0,1:T(2,128)S(1)} collective-permute-done((s32[16,2]{0,1:T(2,128)S(1)}, s32[16,2]{0,1:T(2,128)S(1)}, u32[]{:S(2)}, u32[]{:S(2)}) %collective-permute-start.3) | collective-permute-done | bytes 160 | tf_op jit(solution)/shard_map/ppermute | solution.py:31
  49.8 4.1 %collective-permute-done.4 = s32[16,2]{0,1:T(2,128)S(1)} collective-permute-done((s32[16,2]{0,1:T(2,128)S(1)}, s32[16,2]{0,1:T(2,128)S(1)}, u32[]{:S(2)}, u32[]{:S(2)}) %collective-permute-start.4) | collective-permute-done | bytes 160 | tf_op jit(solution)/shard_map/ppermute | solution.py:31
  53.9 4.2 %collective-permute-done.5 = s32[16,2]{0,1:T(2,128)S(1)} collective-permute-done((s32[16,2]{0,1:T(2,128)S(1)}, s32[16,2]{0,1:T(2,128)S(1)}, u32[]{:S(2)}, u32[]{:S(2)}) %collective-permute-start.5) | collective-permute-done | bytes 160 | tf_op jit(solution)/shard_map/ppermute | solution.py:31
  58.1 4.6 %collective-permute-done.6 = s32[16,2]{0,1:T(2,128)S(1)} collective-permute-done((s32[16,2]{0,1:T(2,128)S(1)}, s32[16,2]{0,1:T(2,128)S(1)}, u32[]{:S(2)}, u32[]{:S(2)}) %collective-permute-start.6) | collective-permute-done | bytes 160 | tf_op jit(solution)/shard_map/ppermute | solution.py:31
  62.7 4.8 %collective-permute-done.7 = s32[16,2]{0,1:T(2,128)S(1)} collective-permute-done((s32[16,2]{0,1:T(2,128)S(1)}, s32[16,2]{0,1:T(2,128)S(1)}, u32[]{:S(2)}, u32[]{:S(2)}) %collective-permute-start.7) | collective-permute-done | bytes 160 | tf_op jit(solution)/shard_map/ppermute | solution.py:31
  67.6 6.4 %collective-permute-done.8 = s32[16,2]{0,1:T(2,128)S(1)} collective-permute-done((s32[16,2]{0,1:T(2,128)S(1)}, s32[16,2]{0,1:T(2,128)S(1)}, u32[]{:S(2)}, u32[]{:S(2)}) %collective-permute-start.8) | collective-permute-done | bytes 160 | tf_op jit(solution)/shard_map/ppermute | solution.py:31
  74.0 5.8 %collective-permute-done.9 = s32[16,2]{0,1:T(2,128)S(1)} collective-permute-done((s32[16,2]{0,1:T(2,128)S(1)}, s32[16,2]{0,1:T(2,128)S(1)}, u32[]{:S(2)}, u32[]{:S(2)}) %collective-permute-start.9) | collective-permute-done | bytes 160 | tf_op jit(solution)/shard_map/ppermute | solution.py:31
  79.8 6.2 %collective-permute-done.10 = s32[16,2]{0,1:T(2,128)S(1)} collective-permute-done((s32[16,2]{0,1:T(2,128)S(1)}, s32[16,2]{0,1:T(2,128)S(1)}, u32[]{:S(2)}, u32[]{:S(2)}) %collective-permute-start.10) | collective-permute-done | bytes 160 | tf_op jit(solution)/shard_map/ppermute | solution.py:31
  86.0 5.1 %collective-permute-done.11 = s32[16,2]{0,1:T(2,128)S(1)} collective-permute-done((s32[16,2]{0,1:T(2,128)S(1)}, s32[16,2]{0,1:T(2,128)S(1)}, u32[]{:S(2)}, u32[]{:S(2)}) %collective-permute-start.11) | collective-permute-done | bytes 160 | tf_op jit(solution)/shard_map/ppermute | solution.py:31
  91.2 5.7 %collective-permute-done.12 = s32[16,2]{0,1:T(2,128)S(1)} collective-permute-done((s32[16,2]{0,1:T(2,128)S(1)}, s32[16,2]{0,1:T(2,128)S(1)}, u32[]{:S(2)}, u32[]{:S(2)}) %collective-permute-start.12) | collective-permute-done | bytes 160 | tf_op jit(solution)/shard_map/ppermute | solution.py:31
  96.9 6.0 %collective-permute-done.13 = s32[16,2]{0,1:T(2,128)S(1)} collective-permute-done((s32[16,2]{0,1:T(2,128)S(1)}, s32[16,2]{0,1:T(2,128)S(1)}, u32[]{:S(2)}, u32[]{:S(2)}) %collective-permute-start.13) | collective-permute-done | bytes 160 | tf_op jit(solution)/shard_map/ppermute | solution.py:31
  102.9 6.0 %collective-permute-done.14 = s32[16,2]{0,1:T(2,128)S(1)} collective-permute-done((s32[16,2]{0,1:T(2,128)S(1)}, s32[16,2]{0,1:T(2,128)S(1)}, u32[]{:S(2)}, u32[]{:S(2)}) %collective-permute-start.14) | collective-permute-done | bytes 160 | tf_op jit(solution)/shard_map/ppermute | solution.py:31
  109.9 13.3 %fusion.1 = f32[256,7168]{1,0:T(8,128)} fusion(bf16[1,512,7168]{2,1,0:T(8,128)(2,1)} %param.9, f32[256]{0:T(256)S(1)} %fusion.14, bf16[256,7168]{1,0:T(8,128)(2,1)} %all-gather.3.cloned.1.call-done, bf16[1,512,7168]{2,1,0:T(8,128)(2,1)} %param.8), kind=kOutput, calls=%fused_computation.2 | convolution fusion | flops 3764256768 | bytes 25691136 | tf_op jit(solution)/shard_map/dot_general | solution.py:41
  123.2 199.2 %reduce-scatter.2.cloned.1.call-done = f32[16,7168]{1,0:T(8,128)} async-done(((f32[256,7168]{1,0:T(8,128)}), f32[16,7168]{1,0:T(8,128)}) %reduce-scatter.2.cloned.1.call-update) | async-done | bytes 458768 | tf_op jit(solution)/shard_map/reduce_scatter | solution.py:43
  322.5 1.1 fusion.12
  323.5 1.1 collective-permute-start.15
  324.6 1.1 collective-permute-done.15
  (28 shorter events, 3.4 us)
Async XLA Ops:
  6.5 103.3 %all-gather.3.cloned.1.call-start = ((), (), s32[]{:S(2)}) async-start(), calls=%async_computation.1 | async-start | bytes 3899392 | tf_op jit(solution)/shard_map/all_gather | solution.py:28
  10.2 312.2 %reduce-scatter.2.cloned.1.call-start = ((), (), s32[]{:S(2)}) async-start(), calls=%async_computation.2 | async-start | bytes 7798784 | tf_op jit(solution)/shard_map/reduce_scatter | solution.py:43
  10.3 26.2 %collective-permute-start = (s32[16,2]{0,1:T(2,128)}, s32[16,2]{0,1:T(2,128)S(1)}, u32[]{:S(2)}, u32[]{:S(2)}) collective-permute-start(s32[16,2]{0,1:T(2,128)} %bitcast.23), channel_id=1, source_target_pairs={{0,1},{1,2},{2,3},{3,4},{4,5},{5,6},{6,7},{7,8},{8,9},{9,10},{10,1... | collective-permute-start | bytes 392 | tf_op jit(solution)/shard_map/ppermute | solution.py:31
  36.5 5.1 %collective-permute-start.1 = (s32[16,2]{0,1:T(2,128)S(1)}, s32[16,2]{0,1:T(2,128)S(1)}, u32[]{:S(2)}, u32[]{:S(2)}) collective-permute-start(s32[16,2]{0,1:T(2,128)S(1)} %collective-permute-done), channel_id=1, source_target_pairs={{0,1},{1,2},{2,3},{3,4},{4,5},{5,6},{6,7},{7,8},{8,9},{9,10},{10,1... | collective-permute-start | bytes 392 | tf_op jit(solution)/shard_map/ppermute | solution.py:31
  41.6 4.2 %collective-permute-start.2 = (s32[16,2]{0,1:T(2,128)S(1)}, s32[16,2]{0,1:T(2,128)S(1)}, u32[]{:S(2)}, u32[]{:S(2)}) collective-permute-start(s32[16,2]{0,1:T(2,128)S(1)} %collective-permute-done.1), channel_id=1, source_target_pairs={{0,1},{1,2},{2,3},{3,4},{4,5},{5,6},{6,7},{7,8},{8,9},{9,10},{10,1... | collective-permute-start | bytes 392 | tf_op jit(solution)/shard_map/ppermute | solution.py:31
  45.8 4.0 %collective-permute-start.3 = (s32[16,2]{0,1:T(2,128)S(1)}, s32[16,2]{0,1:T(2,128)S(1)}, u32[]{:S(2)}, u32[]{:S(2)}) collective-permute-start(s32[16,2]{0,1:T(2,128)S(1)} %collective-permute-done.2), channel_id=1, source_target_pairs={{0,1},{1,2},{2,3},{3,4},{4,5},{5,6},{6,7},{7,8},{8,9},{9,10},{10,1... | collective-permute-start | bytes 392 | tf_op jit(solution)/shard_map/ppermute | solution.py:31
  49.8 4.1 %collective-permute-start.4 = (s32[16,2]{0,1:T(2,128)S(1)}, s32[16,2]{0,1:T(2,128)S(1)}, u32[]{:S(2)}, u32[]{:S(2)}) collective-permute-start(s32[16,2]{0,1:T(2,128)S(1)} %collective-permute-done.3), channel_id=1, source_target_pairs={{0,1},{1,2},{2,3},{3,4},{4,5},{5,6},{6,7},{7,8},{8,9},{9,10},{10,1... | collective-permute-start | bytes 392 | tf_op jit(solution)/shard_map/ppermute | solution.py:31
  53.9 4.2 %collective-permute-start.5 = (s32[16,2]{0,1:T(2,128)S(1)}, s32[16,2]{0,1:T(2,128)S(1)}, u32[]{:S(2)}, u32[]{:S(2)}) collective-permute-start(s32[16,2]{0,1:T(2,128)S(1)} %collective-permute-done.4), channel_id=1, source_target_pairs={{0,1},{1,2},{2,3},{3,4},{4,5},{5,6},{6,7},{7,8},{8,9},{9,10},{10,1... | collective-permute-start | bytes 392 | tf_op jit(solution)/shard_map/ppermute | solution.py:31
  58.1 4.6 %collective-permute-start.6 = (s32[16,2]{0,1:T(2,128)S(1)}, s32[16,2]{0,1:T(2,128)S(1)}, u32[]{:S(2)}, u32[]{:S(2)}) collective-permute-start(s32[16,2]{0,1:T(2,128)S(1)} %collective-permute-done.5), channel_id=1, source_target_pairs={{0,1},{1,2},{2,3},{3,4},{4,5},{5,6},{6,7},{7,8},{8,9},{9,10},{10,1... | collective-permute-start | bytes 392 | tf_op jit(solution)/shard_map/ppermute | solution.py:31
  62.7 4.8 %collective-permute-start.7 = (s32[16,2]{0,1:T(2,128)S(1)}, s32[16,2]{0,1:T(2,128)S(1)}, u32[]{:S(2)}, u32[]{:S(2)}) collective-permute-start(s32[16,2]{0,1:T(2,128)S(1)} %collective-permute-done.6), channel_id=1, source_target_pairs={{0,1},{1,2},{2,3},{3,4},{4,5},{5,6},{6,7},{7,8},{8,9},{9,10},{10,1... | collective-permute-start | bytes 392 | tf_op jit(solution)/shard_map/ppermute | solution.py:31
  67.6 6.4 %collective-permute-start.8 = (s32[16,2]{0,1:T(2,128)S(1)}, s32[16,2]{0,1:T(2,128)S(1)}, u32[]{:S(2)}, u32[]{:S(2)}) collective-permute-start(s32[16,2]{0,1:T(2,128)S(1)} %collective-permute-done.7), channel_id=1, source_target_pairs={{0,1},{1,2},{2,3},{3,4},{4,5},{5,6},{6,7},{7,8},{8,9},{9,10},{10,1... | collective-permute-start | bytes 392 | tf_op jit(solution)/shard_map/ppermute | solution.py:31
  74.0 5.8 %collective-permute-start.9 = (s32[16,2]{0,1:T(2,128)S(1)}, s32[16,2]{0,1:T(2,128)S(1)}, u32[]{:S(2)}, u32[]{:S(2)}) collective-permute-start(s32[16,2]{0,1:T(2,128)S(1)} %collective-permute-done.8), channel_id=1, source_target_pairs={{0,1},{1,2},{2,3},{3,4},{4,5},{5,6},{6,7},{7,8},{8,9},{9,10},{10,1... | collective-permute-start | bytes 392 | tf_op jit(solution)/shard_map/ppermute | solution.py:31
  79.8 6.2 %collective-permute-start.10 = (s32[16,2]{0,1:T(2,128)S(1)}, s32[16,2]{0,1:T(2,128)S(1)}, u32[]{:S(2)}, u32[]{:S(2)}) collective-permute-start(s32[16,2]{0,1:T(2,128)S(1)} %collective-permute-done.9), channel_id=1, source_target_pairs={{0,1},{1,2},{2,3},{3,4},{4,5},{5,6},{6,7},{7,8},{8,9},{9,10},{10,1... | collective-permute-start | bytes 392 | tf_op jit(solution)/shard_map/ppermute | solution.py:31
  86.0 5.1 %collective-permute-start.11 = (s32[16,2]{0,1:T(2,128)S(1)}, s32[16,2]{0,1:T(2,128)S(1)}, u32[]{:S(2)}, u32[]{:S(2)}) collective-permute-start(s32[16,2]{0,1:T(2,128)S(1)} %collective-permute-done.10), channel_id=1, source_target_pairs={{0,1},{1,2},{2,3},{3,4},{4,5},{5,6},{6,7},{7,8},{8,9},{9,10},{10,1... | collective-permute-start | bytes 392 | tf_op jit(solution)/shard_map/ppermute | solution.py:31
  91.1 5.8 %collective-permute-start.12 = (s32[16,2]{0,1:T(2,128)S(1)}, s32[16,2]{0,1:T(2,128)S(1)}, u32[]{:S(2)}, u32[]{:S(2)}) collective-permute-start(s32[16,2]{0,1:T(2,128)S(1)} %collective-permute-done.11), channel_id=1, source_target_pairs={{0,1},{1,2},{2,3},{3,4},{4,5},{5,6},{6,7},{7,8},{8,9},{9,10},{10,1... | collective-permute-start | bytes 392 | tf_op jit(solution)/shard_map/ppermute | solution.py:31
  96.9 6.0 %collective-permute-start.13 = (s32[16,2]{0,1:T(2,128)S(1)}, s32[16,2]{0,1:T(2,128)S(1)}, u32[]{:S(2)}, u32[]{:S(2)}) collective-permute-start(s32[16,2]{0,1:T(2,128)S(1)} %collective-permute-done.12), channel_id=1, source_target_pairs={{0,1},{1,2},{2,3},{3,4},{4,5},{5,6},{6,7},{7,8},{8,9},{9,10},{10,1... | collective-permute-start | bytes 392 | tf_op jit(solution)/shard_map/ppermute | solution.py:31
  102.9 6.0 %collective-permute-start.14 = (s32[16,2]{0,1:T(2,128)S(1)}, s32[16,2]{0,1:T(2,128)S(1)}, u32[]{:S(2)}, u32[]{:S(2)}) collective-permute-start(s32[16,2]{0,1:T(2,128)S(1)} %collective-permute-done.13), channel_id=1, source_target_pairs={{0,1},{1,2},{2,3},{3,4},{4,5},{5,6},{6,7},{7,8},{8,9},{9,10},{10,1... | collective-permute-start | bytes 392 | tf_op jit(solution)/shard_map/ppermute | solution.py:31
  123.2 199.2 %copy-start = (bf16[1,16,7168]{2,1,0:T(8,128)(2,1)S(1)}, bf16[1,16,7168]{2,1,0:T(8,128)(2,1)}, u32[]{:S(2)}) copy-start(bf16[1,16,7168]{2,1,0:T(8,128)(2,1)} %param.6) | copy-start | bytes 688132
  323.5 2.2 collective-permute-start.15
Sparse Core Ops, SparseCore 0:
  10.3 72.1 all-gather.2
  123.4 199.0 reduce-scatter.1
